TPU v7x, 32 devices: a whole 2x2x4 slice. The times are simulated.
32 devices in a mesh: ctx: 8 (over z, y), tp: 4 (over x, core).
Axes of the slice: x: 2, y: 2, z: 4, core: 2. Of those that a mesh axis runs over, the one named last changes fastest.
Arguments:
- tokens: bfloat16 [6144, 4096], P('ctx'), may hold values from -6 to 6
- in_weight: bfloat16 [4096, 3, 4096], P('ctx', None, 'tp'), may hold values from -0.09375 to 0.09375
- short_taps: float32 [3, 4096, 7], P(None, 'tp'), may hold values from -2.5 to 2.5
- medium_taps: float32 [4096, 128], P('tp'), may hold values from -2 to 2
- medium_decay: float32 [4096], P('tp'), may hold values from 0.01 to 0.3
- skip_gain: float32 [4096], P('tp'), may hold values from 0.5 to 1.5
- out_weight: bfloat16 [4096, 4096], P('tp'), may hold values from -0.09375 to 0.09375
Outputs:
- mixed: bfloat16 [6144, 4096], P('ctx', 'tp')
All inputs are finite; a program needn't handle non-finite values.
Results may differ from a plain program's by a relative error of at most 0.0072.
Values may be sent and summed in bfloat16 or wider, within the bound.
No kernel may reach another device: no remote copies, remote signals or barrier semaphores. Data moves between devices by JAX's collectives and lax.ppermute only.
A program may use at most 192 MiB of HBM per device.

v0:
```python
import jax
import jax.numpy as jnp
from jax import lax
from jax.sharding import PartitionSpec as P


def skewed(extended):
    group_size = extended.shape[0]
    width = extended.shape[1] // 2
    reverse = extended[:, ::-1]
    tiled = jnp.tile(reverse, (1, width))
    flat = tiled[:, width - 1 : width - 1 + width * (2 * width - 1)]
    return flat.reshape(group_size, width, 2 * width - 1)[:, :, :width]


def toeplitz_pair(filters):
    blank = jnp.zeros(filters.shape, jnp.float32)
    lower = skewed(jnp.concatenate([blank, filters], axis=1))
    upper = skewed(jnp.concatenate([filters, blank], axis=1))
    return (lower, upper)


def channel_filter(fields, short_weights, filters, skip_weights):
    group_size = fields.shape[1]
    length = fields.shape[2]
    short_count = short_weights.shape[2]
    medium_count = filters.shape[1]
    widened = jnp.pad(fields.astype(jnp.float32), ((0, 0), (0, 0), (short_count - 1, 0)))
    smoothed = jnp.zeros(fields.shape, jnp.float32)
    for lag_step in range(short_count):
        start_col = short_count - 1 - lag_step
        smoothed = (
            smoothed
            + short_weights[:, :, lag_step : lag_step + 1]
            * widened[:, :, start_col : start_col + length]
        )
    product = smoothed[1] * smoothed[2]
    blocks = product.reshape(group_size, -1, medium_count)
    earlier = jnp.concatenate(
        [jnp.zeros((group_size, 1, medium_count), jnp.float32), blocks[:, :-1]], axis=1
    )
    lower, upper = toeplitz_pair(filters)
    response = jnp.einsum("cbj,cij->cbi", blocks, lower, precision=lax.Precision.HIGHEST)
    response = response + jnp.einsum(
        "cbj,cij->cbi", earlier, upper, precision=lax.Precision.HIGHEST
    )
    response = response.reshape(group_size, -1)
    return (smoothed[0] * (response + skip_weights[:, None] * product)).astype(jnp.bfloat16)


def per_device(tokens, in_weight, short_taps, medium_taps, medium_decay, skip_gain, out_weight):
    row_count = tokens.shape[0]
    channel_count = in_weight.shape[2]
    ctx_count = lax.axis_size("ctx")
    group_size = channel_count // ctx_count
    medium_count = medium_taps.shape[1]
    features = jnp.einsum(
        "rd,dkc->rkc",
        tokens,
        lax.all_gather(in_weight, "ctx", axis=0, tiled=True),
        preferred_element_type=jnp.float32,
    ).astype(jnp.bfloat16)
    lag_values = lax.broadcasted_iota(jnp.float32, (1, medium_count), 1)
    filters = medium_taps * jnp.exp(-medium_decay[:, None] * lag_values)
    tilted = jnp.transpose(features, (1, 2, 0))
    spread = lax.all_to_all(tilted, "ctx", split_axis=1, concat_axis=2, tiled=True)
    offset = lax.axis_index("ctx") * group_size
    short_local = lax.dynamic_slice_in_dim(short_taps, offset, group_size, 1)
    filter_local = lax.dynamic_slice_in_dim(filters, offset, group_size, 0)
    skip_local = lax.dynamic_slice_in_dim(skip_gain, offset, group_size, 0)
    filtered = channel_filter(spread, short_local, filter_local, skip_local)
    filtered = filtered.reshape(group_size, ctx_count, row_count)
    returned = lax.all_to_all(filtered, "ctx", split_axis=1, concat_axis=0, tiled=True)
    gated = returned.reshape(channel_count, row_count)
    summed = lax.psum_scatter(
        lax.dot_general(
            out_weight, gated, (((0,), (0,)), ((), ())), preferred_element_type=jnp.float32
        ),
        "tp",
        scatter_dimension=0,
        tiled=True,
    )
    return jnp.transpose(summed).astype(jnp.bfloat16)


def solution(mesh):
    return jax.shard_map(
        per_device,
        mesh=mesh,
        in_specs=(
            P("ctx", None),
            P("ctx", None, "tp"),
            P(None, "tp", None),
            P("tp", None),
            P("tp"),
            P("tp"),
            P("tp", None),
        ),
        out_specs=P("ctx", "tp"),
        check_vma=False,
    )
```

profile of v0, /device:TPU:0, one launch (start us, length us, event | category | flops | bytes accessed | tf_op | source)
XLA Modules:
  0.0 935.4 jit_solution(1060447155559455234)
XLA Ops:
  6.5 4.7 copy.21
  11.3 483.3 %all-gather.2.cloned.1.call-done = bf16[4096,3,1024]{0,2,1:T(8,128)(2,1)} async-done(((bf16[512,3,1024]{0,2,1:T(8,128)(2,1)}), bf16[4096,3,1024]{0,2,1:T(8,128)(2,1)}) %all-gather.2.cloned.1.call-update) | async-done | bytes 25165840 | tf_op jit(solution)/shard_map/all_gather | solution.py:60
  494.6 24.9 %fusion.9 = bf16[3,1024,768]{2,1,0:T(8,128)(2,1)S(1)} fusion(bf16[4096,3,1024]{0,2,1:T(8,128)(2,1)} %all-gather.2.cloned.1.call-done, bf16[768,4096]{1,0:T(8,128)(2,1)} %param.7), kind=kOutput, calls=%fused_computation.14 | convolution fusion | flops 19329712128 | bytes 36175872 | tf_op jit(solution)/shard_map/rd,dkc->rkc/dot_general | solution.py:57
  519.5 6.6 copy.22
  526.1 4.9 all-to-all-start
  536.1 20.7 %copy.38 = f32[16,8,128,256]{3,1,2,0:T(8,128)S(1)} copy(f32[16,8,128,256]{3,2,1,0:T(8,128)S(1)} %bitcast.46) | data formatting | bytes 33554432
  556.8 7.5 slice.91
  564.2 28.9 %reshape.44 = f32[128,128,255]{2,1,0:T(8,128)} reshape(f32[128,32640]{1,0:T(8,128)} %slice.91) | data formatting | bytes 33423360 | tf_op jit(solution)/shard_map/reshape | solution.py:13
  594.5 20.7 %copy.37 = f32[16,8,128,256]{3,1,2,0:T(8,128)S(1)} copy(f32[16,8,128,256]{3,2,1,0:T(8,128)S(1)} %bitcast.47) | data formatting | bytes 33554432
  615.1 7.6 slice.88
  622.7 28.9 %reshape.43 = f32[128,128,255]{2,1,0:T(8,128)} reshape(f32[128,32640]{1,0:T(8,128)} %slice.88) | data formatting | bytes 33423360 | tf_op jit(solution)/shard_map/reshape | solution.py:13
  651.6 17.8 %all-to-all-done = bf16[3,1024,768]{2,0,1:T(4,128)(2,1)} async-done(((bf16[3,1024,768]{2,0,1:T(4,128)(2,1)}), bf16[3,1024,768]{2,0,1:T(4,128)(2,1)}, u32[]{:S(2)}, u32[]{:S(2)}) %all-to-all-start) | async-done | bytes 4718624 | tf_op jit(solution)/shard_map/all_to_all | solution.py:66
  672.8 4.8 convert_bitcast_fusion
  677.6 9.6 %copy.24 = f32[3,128,8,768]{1,3,2,0:T(8,128)} copy(f32[3,128,8,768]{3,1,2,0:T(8,128)} %convert_bitcast_fusion) | data formatting | bytes 18874368 | tf_op jit(solution)/shard_map/convert_element_type | solution.py:28
  687.2 30.6 %multiply_add_fusion = f32[3,128,6144]{1,2,0:T(8,128)} fusion(f32[3,128,6144]{1,2,0:T(8,128)} %bitcast.50, f32[3,128]{1,0:T(4,128)S(1)} %get-tuple-element.16, f32[3,128]{1,0:T(4,128)S(1)} %get-tuple-element.17, f32[3,128]{1,0:T(4,128)S(1)} %get-tuple-element.18, f32[3,128]{1,0:T(4,128)S(1)} %get-tuple-element.19, f32[3,128]{1,0:T(4,128)S(1)} %get-tuple-element.20, ...), kind=kLoop, calls=%fused_computation.1 | loop fusion | flops 30670848 | bytes 18885120 | tf_op jit(solution)/shard_map/add | solution.py:33
  717.8 5.9 slice_multiply_fusion
  723.7 3.5 copy.28
  731.9 16.0 %fusion = f32[128,48,128]{2,1,0:T(8,128)S(1)} fusion(f32[128,128,255]{2,1,0:T(8,128)} %reshape.44, f32[128,47,128]{2,1,0:T(8,128)} %bitcast.53), kind=kOutput, calls=%fused_computation.2 | convolution fusion | flops 1207959552 | bytes 14680064 | tf_op jit(solution)/shard_map/cbj,cij->cbi/dot_general | solution.py:44
  747.9 17.1 %fusion.12 = f32[128,48,128]{2,1,0:T(8,128)} fusion(f32[128,48,128]{2,1,0:T(8,128)S(1)} %fusion, f32[128,48,128]{2,1,0:T(8,128)S(1)} %copy-done, f32[128,128,255]{2,1,0:T(8,128)} %reshape.43), kind=kOutput, calls=%fused_computation.15 | convolution fusion | flops 1208745984 | bytes 17825792 | tf_op jit(solution)/shard_map/cbj,cij->cbi/dot_general | solution.py:43
  765.0 4.6 reshape.45
  769.7 4.1 fusion.7
  773.7 40.5 %all_to_all.24 = bf16[128,8,768]{2,0,1:T(8,128)(2,1)S(1)} all-to-all(bf16[128,8,768]{2,0,1:T(8,128)(2,1)S(1)} %fusion.7), channel_id=1, replica_groups=mesh['ctx'=8,'tp'=4] {'ctx'}, dimensions={1} | all-to-all | bytes 3145728 | tf_op jit(solution)/shard_map/all_to_all | solution.py:73
  814.3 12.5 %convolution_bitcast_fusion = f32[4096,768]{0,1:T(8,128)} fusion(bf16[1024,768]{1,0:T(8,128)(2,1)S(1)} %bitcast.56, bf16[1024,4096]{1,0:T(8,128)(2,1)} %param.13), kind=kOutput, calls=%fused_computation.6 | convolution fusion | flops 6442450944 | bytes 22544384 | tf_op jit(solution)/shard_map/dot_general | solution.py:76
  826.8 98.2 %reduce-scatter.2.cloned.1.call-done = f32[1024,768]{0,1:T(8,128)} async-done(((f32[4096,768]{0,1:T(8,128)}), f32[1024,768]{0,1:T(8,128)}) %reduce-scatter.2.cloned.1.call-update) | async-done | bytes 3145744 | tf_op jit(solution)/shard_map/reduce_scatter | solution.py:75
  (28 shorter events, 17.8 us)
Async XLA Ops:
  6.5 488.0 %all-gather.2.cloned.1.call-start = ((), (), s32[]{:S(2)}) async-start(), calls=%async_computation.3 | async-start | bytes 28311552 | tf_op jit(solution)/shard_map/all_gather | solution.py:60
  526.1 4.9 copy-start.2
  526.1 143.3 %all-to-all-start = ((bf16[3,1024,768]{2,0,1:T(4,128)(2,1)}), bf16[3,1024,768]{2,0,1:T(4,128)(2,1)}, u32[]{:S(2)}, u32[]{:S(2)}) async-start(bf16[3,1024,768]{2,0,1:T(4,128)(2,1)} %copy.22), calls=%async_computation | async-start | bytes 12582912 | tf_op jit(solution)/shard_map/all_to_all | solution.py:66
  531.0 394.1 %reduce-scatter.2.cloned.1.call-start = ((), (), s32[]{:S(2)}) async-start(), calls=%async_computation.4 | async-start | bytes 15728640 | tf_op jit(solution)/shard_map/reduce_scatter | solution.py:75
  731.9 16.0 %copy-start = (f32[128,48,128]{2,1,0:T(8,128)S(1)}, f32[128,48,128]{2,1,0:T(8,128)}, u32[]{:S(2)}) copy-start(f32[128,48,128]{2,1,0:T(8,128)} %copy.29) | copy-start | bytes 9437188
  747.9 21.7 %copy-start.1 = (f32[128,8,768]{2,0,1:T(8,128)S(1)}, f32[128,8,768]{2,0,1:T(8,128)}, u32[]{:S(2)}) copy-start(f32[128,8,768]{2,0,1:T(8,128)} %copy.28) | copy-start | bytes 9437188
Sparse Core Ops, SparseCore 0:
  11.4 483.1 all-gather.1
  827.0 98.0 reduce-scatter.1
where the time goes:
time: 943 us; the launch traced here: 935 us
  waiting for transfers between devices  599 us (64%)
  local copies, waits for them, and re-layouts  157 us (17%)
  matrix products  70.6 us (7%)
  other arithmetic  49.5 us (5%)
  blocking collectives  40.5 us (4%)
  between operations  13.8 us (1%)
    all_gather x1, waiting for transfers between devices, per_device(): lax.all_gather(in_weight, 'ctx', axis=0, tiled=True)  483 us
    reduce_scatter x1, waiting for transfers between devices, per_device(): lax.psum_scatter(lax.dot_general(out_weight, gated, (((0,), (0,)), ((), (...  98.2 us
    reshape x2, local copies, waits for them, and re-layouts, skewed(): return flat.reshape(group_size, width, 2 * width - 1)[:, :, :width]  57.8 us
    unnamed x13, local copies, waits for them, and re-layouts  46.1 us
    all_to_all x1, blocking collectives, per_device(): lax.all_to_all(filtered, 'ctx', split_axis=1, concat_axis=0, tiled=True)  40.5 us
    add x1, other arithmetic, channel_filter(): smoothed + short_weights[:, :, lag_step:lag_step + 1] * widened[:, :, sta...  30.6 us
    dot_general x1, matrix products, per_device(): jnp.einsum('rd,dkc->rkc', tokens, lax.all_gather(in_weight, 'ctx', axis=0...  24.9 us
  transfers between devices with their start and end apart: 3, of which 3 were waited for; matrix products, arithmetic and copies ran while one was open for 13% of the time, Pallas kernels for 0%

commit v1 on v0

--- a/solution.py
+++ b/solution.py
@@ -2,6 +2,27 @@
 import jax.numpy as jnp
 from jax import lax
 from jax.sharding import PartitionSpec as P
+
+
+def gather_around(value, axis, dim):
+    peers, here, rows = (lax.axis_size(axis), lax.axis_index(axis), value.shape[dim])
+    ahead = [(i, (i + 1) % peers) for i in range(peers)]
+    left = [(i, (i - 1) % peers) for i in range(peers)]
+    out = jnp.zeros((*value.shape[:dim], peers * rows, *value.shape[dim + 1 :]), value.dtype)
+    out = lax.dynamic_update_slice_in_dim(out, value, here * rows, axis=dim)
+    from_left = from_right = value
+    half = peers // 2
+    for step in range(1, half + 1):
+        from_left = lax.ppermute(from_left, axis, ahead)
+        out = lax.dynamic_update_slice_in_dim(
+            out, from_left, (here - step) % peers * rows, axis=dim
+        )
+        if step < peers - half:
+            from_right = lax.ppermute(from_right, axis, left)
+            out = lax.dynamic_update_slice_in_dim(
+                out, from_right, (here + step) % peers * rows, axis=dim
+            )
+    return out
 
 
 def skewed(extended):
@@ -57,7 +78,7 @@
     features = jnp.einsum(
         "rd,dkc->rkc",
         tokens,
-        lax.all_gather(in_weight, "ctx", axis=0, tiled=True),
+        gather_around(in_weight, "ctx", 0),
         preferred_element_type=jnp.float32,
     ).astype(jnp.bfloat16)
     lag_values = lax.broadcasted_iota(jnp.float32, (1, medium_count), 1)

time: 943 us -> 953 us (1.011)
  waiting for transfers between devices: 599 us -> 521 us
  local copies, waits for them, and re-layouts: 157 us -> 213 us
  starting transfers between devices: 4.91 us -> 24.5 us
  matrix products: 70.6 us -> 82.1 us
    all_gather x1 -> x0, waiting for transfers between devices: 483 us -> none  [per_device(): lax.all_gather(in_weight, 'ctx', axis=0, tiled=True)]
    ppermute x0 -> x7, waiting for transfers between devices: none -> 408 us  [the longest x4 408 us: gather_around(): from_left = lax.ppermute(from_left, axis, ahead)]
    ppermute x0 -> x7, local copies, waits for them, and re-layouts: none -> 26.7 us  [the longest x4 15.7 us: gather_around(): from_left = lax.ppermute(from_left, axis, ahead)]
    ppermute x0 -> x7, starting transfers between devices: none -> 19.6 us  [the longest x4 10.4 us: gather_around(): from_left = lax.ppermute(from_left, axis, ahead)]
    dynamic_update_slice x0 -> x8, local copies, waits for them, and re-layouts: none -> 19.2 us  [the longest x4 11.5 us: gather_around(): lax.dynamic_update_slice_in_dim(out, from_left, (here - step) % peers * r...]
    dot_general x1, matrix products: 24.9 us -> 36.5 us  [per_device(): jnp.einsum('rd,dkc->rkc', tokens, gather_around(in_weight, 'ctx', 0), pre...]
    unnamed x13 -> x21, local copies, waits for them, and re-layouts: 46.1 us -> 47.3 us
  transfers between devices with their start and end apart: 3 -> 9, of which waited for: 3 -> 6; matrix products, arithmetic and copies ran while one was open for 13% -> 18% of each run, Pallas kernels for 0% -> 0%
where the time goes in v1:
time: 953 us; the launch traced here: 945 us
  waiting for transfers between devices  521 us (55%)
  local copies, waits for them, and re-layouts  213 us (22%)
  matrix products  82.1 us (9%)
  other arithmetic  49.4 us (5%)
  blocking collectives  40.6 us (4%)
  starting transfers between devices  24.5 us (3%)
  between operations  14.2 us (1%)
    ppermute x4, waiting for transfers between devices, gather_around(): from_left = lax.ppermute(from_left, axis, ahead)  408 us
    reduce_scatter x1, waiting for transfers between devices, per_device(): lax.psum_scatter(lax.dot_general(out_weight, gated, (((0,), (0,)), ((), (...  98.3 us
    reshape x2, local copies, waits for them, and re-layouts, skewed(): return flat.reshape(group_size, width, 2 * width - 1)[:, :, :width]  57.8 us
    unnamed x21, local copies, waits for them, and re-layouts  47.3 us
    all_to_all x1, blocking collectives, per_device(): lax.all_to_all(filtered, 'ctx', split_axis=1, concat_axis=0, tiled=True)  40.6 us
    dot_general x1, matrix products, per_device(): jnp.einsum('rd,dkc->rkc', tokens, gather_around(in_weight, 'ctx', 0), pre...  36.5 us
    add x1, other arithmetic, channel_filter(): smoothed + short_weights[:, :, lag_step:lag_step + 1] * widened[:, :, sta...  30.4 us
  transfers between devices with their start and end apart: 9, of which 6 were waited for; matrix products, arithmetic and copies ran while one was open for 18% of the time, Pallas kernels for 0%

profile of v1, /device:TPU:0, one launch (start us, length us, event | category | flops | bytes accessed | tf_op | source)
XLA Modules:
  0.0 945.0 jit_solution(18441965568147669737)
XLA Ops:
  12.5 132.0 %collective-permute-done = bf16[512,3,1024]{2,0,1:T(8,128)(2,1)S(1)} collective-permute-done((bf16[512,3,1024]{2,0,1:T(8,128)(2,1)}, bf16[512,3,1024]{2,0,1:T(8,128)(2,1)S(1)}, u32[]{:S(2)}, u32[]{:S(2)}) %collective-permute-start) | collective-permute-done | bytes 3145760 | tf_op jit(solution)/shard_map/ppermute | solution.py:16
  150.1 130.8 %collective-permute-done.2 = bf16[512,3,1024]{2,0,1:T(8,128)(2,1)S(1)} collective-permute-done((bf16[512,3,1024]{2,0,1:T(8,128)(2,1)S(1)}, bf16[512,3,1024]{2,0,1:T(8,128)(2,1)S(1)}, u32[]{:S(2)}, u32[]{:S(2)}) %collective-permute-start.2) | collective-permute-done | bytes 3145760 | tf_op jit(solution)/shard_map/ppermute | solution.py:16
  288.0 130.1 %collective-permute-done.4 = bf16[512,3,1024]{2,0,1:T(8,128)(2,1)} collective-permute-done((bf16[512,3,1024]{2,0,1:T(8,128)(2,1)S(1)}, bf16[512,3,1024]{2,0,1:T(8,128)(2,1)}, u32[]{:S(2)}, u32[]{:S(2)}) %collective-permute-start.4) | collective-permute-done | bytes 3145760 | tf_op jit(solution)/shard_map/ppermute | solution.py:16
  424.0 8.5 broadcast_in_dim.2
  474.5 15.2 %collective-permute-done.6 = bf16[512,3,1024]{2,0,1:T(8,128)(2,1)} collective-permute-done((bf16[512,3,1024]{2,0,1:T(8,128)(2,1)}, bf16[512,3,1024]{2,0,1:T(8,128)(2,1)}, u32[]{:S(2)}, u32[]{:S(2)}) %collective-permute-start.6) | collective-permute-done | bytes 3145760 | tf_op jit(solution)/shard_map/ppermute | solution.py:16
  494.8 36.5 %fusion.9 = bf16[3,1024,768]{2,1,0:T(8,128)(2,1)S(1)} fusion(bf16[4096,3,1024]{0,2,1:T(8,128)(2,1)} %constant_dynamic-update-slice_fusion, bf16[768,4096]{1,0:T(8,128)(2,1)} %param.7), kind=kOutput, calls=%fused_computation.14 | convolution fusion | flops 19329712128 | bytes 36175872 | tf_op jit(solution)/shard_map/rd,dkc->rkc/dot_general | solution.py:78
  531.4 6.6 copy.50
  538.0 4.9 all-to-all-start
  546.8 20.7 %copy.66 = f32[16,8,128,256]{3,1,2,0:T(8,128)S(1)} copy(f32[16,8,128,256]{3,2,1,0:T(8,128)S(1)} %bitcast.46) | data formatting | bytes 33554432
  567.5 7.5 slice.91
  575.0 28.9 %reshape.44 = f32[128,128,255]{2,1,0:T(8,128)} reshape(f32[128,32640]{1,0:T(8,128)} %slice.91) | data formatting | bytes 33423360 | tf_op jit(solution)/shard_map/reshape | solution.py:34
  605.4 20.7 %copy.65 = f32[16,8,128,256]{3,1,2,0:T(8,128)S(1)} copy(f32[16,8,128,256]{3,2,1,0:T(8,128)S(1)} %bitcast.47) | data formatting | bytes 33554432
  626.1 7.6 slice.88
  633.6 28.9 %reshape.43 = f32[128,128,255]{2,1,0:T(8,128)} reshape(f32[128,32640]{1,0:T(8,128)} %slice.88) | data formatting | bytes 33423360 | tf_op jit(solution)/shard_map/reshape | solution.py:34
  663.3 15.0 %all-to-all-done = bf16[3,1024,768]{2,0,1:T(4,128)(2,1)} async-done(((bf16[3,1024,768]{2,0,1:T(4,128)(2,1)}), bf16[3,1024,768]{2,0,1:T(4,128)(2,1)}, u32[]{:S(2)}, u32[]{:S(2)}) %all-to-all-start) | async-done | bytes 4718624 | tf_op jit(solution)/shard_map/all_to_all | solution.py:87
  681.8 4.8 convert_bitcast_fusion
  686.6 9.8 %copy.52 = f32[3,128,8,768]{1,3,2,0:T(8,128)} copy(f32[3,128,8,768]{3,1,2,0:T(8,128)} %convert_bitcast_fusion) | data formatting | bytes 18874368 | tf_op jit(solution)/shard_map/convert_element_type | solution.py:49
  696.3 30.4 %multiply_add_fusion = f32[3,128,6144]{1,2,0:T(8,128)} fusion(f32[3,128,6144]{1,2,0:T(8,128)} %bitcast.50, f32[3,128]{1,0:T(4,128)S(1)} %get-tuple-element.16, f32[3,128]{1,0:T(4,128)S(1)} %get-tuple-element.17, f32[3,128]{1,0:T(4,128)S(1)} %get-tuple-element.18, f32[3,128]{1,0:T(4,128)S(1)} %get-tuple-element.19, f32[3,128]{1,0:T(4,128)S(1)} %get-tuple-element.20, ...), kind=kLoop, calls=%fused_computation.1 | loop fusion | flops 30670848 | bytes 18885120 | tf_op jit(solution)/shard_map/add | solution.py:54
  726.8 5.9 slice_multiply_fusion
  735.1 16.0 %fusion = f32[128,48,128]{2,1,0:T(8,128)S(1)} fusion(f32[128,128,255]{2,1,0:T(8,128)} %reshape.44, f32[128,47,128]{2,1,0:T(8,128)} %bitcast.53), kind=kOutput, calls=%fused_computation.2 | convolution fusion | flops 1207959552 | bytes 14680064 | tf_op jit(solution)/shard_map/cbj,cij->cbi/dot_general | solution.py:65
  751.1 17.0 %fusion.12 = f32[128,48,128]{2,1,0:T(8,128)} fusion(f32[128,48,128]{2,1,0:T(8,128)S(1)} %fusion, f32[128,48,128]{2,1,0:T(8,128)S(1)} %copy-done, f32[128,128,255]{2,1,0:T(8,128)} %reshape.43), kind=kOutput, calls=%fused_computation.15 | convolution fusion | flops 1208745984 | bytes 17825792 | tf_op jit(solution)/shard_map/cbj,cij->cbi/dot_general | solution.py:64
  783.0 40.6 %all_to_all.24 = bf16[128,8,768]{2,0,1:T(8,128)(2,1)S(1)} all-to-all(bf16[128,8,768]{2,0,1:T(8,128)(2,1)S(1)} %fusion.7), channel_id=1, replica_groups=mesh['ctx'=8,'tp'=4] {'ctx'}, dimensions={1} | all-to-all | bytes 3145728 | tf_op jit(solution)/shard_map/all_to_all | solution.py:94
  823.6 12.5 %convolution_bitcast_fusion = f32[4096,768]{0,1:T(8,128)} fusion(bf16[1024,768]{1,0:T(8,128)(2,1)S(1)} %bitcast.56, bf16[1024,4096]{1,0:T(8,128)(2,1)} %param.13), kind=kOutput, calls=%fused_computation.6 | convolution fusion | flops 6442450944 | bytes 22544384 | tf_op jit(solution)/shard_map/dot_general | solution.py:97
  836.1 98.3 %reduce-scatter.2.cloned.1.call-done = f32[1024,768]{0,1:T(8,128)} async-done(((f32[4096,768]{0,1:T(8,128)}), f32[1024,768]{0,1:T(8,128)}) %reduce-scatter.2.cloned.1.call-update) | async-done | bytes 3145744 | tf_op jit(solution)/shard_map/reduce_scatter | solution.py:96
  (63 shorter events, 101.6 us)
Async XLA Ops:
  6.5 138.1 %collective-permute-start = (bf16[512,3,1024]{2,0,1:T(8,128)(2,1)}, bf16[512,3,1024]{2,0,1:T(8,128)(2,1)S(1)}, u32[]{:S(2)}, u32[]{:S(2)}) collective-permute-start(bf16[512,3,1024]{2,0,1:T(8,128)(2,1)} %param.8), channel_id=1, source_target_pairs={{0,4},{4,8},{8,12},{12,16},{16,20},{20,24},{24,28},{28,0},{1,5},{5... | collective-permute-start | bytes 9437192 | tf_op jit(solution)/shard_map/ppermute | solution.py:16
  9.5 137.5 %collective-permute-start.1 = (bf16[512,3,1024]{2,0,1:T(8,128)(2,1)}, bf16[512,3,1024]{2,0,1:T(8,128)(2,1)S(1)}, u32[]{:S(2)}, u32[]{:S(2)}) collective-permute-start(bf16[512,3,1024]{2,0,1:T(8,128)(2,1)} %param.8), channel_id=1, source_target_pairs={{0,28},{4,0},{8,4},{12,8},{16,12},{20,16},{24,20},{28,24},{1,29},{... | collective-permute-start | bytes 9437192 | tf_op jit(solution)/shard_map/ppermute | solution.py:21
  144.6 273.5 %copy-start.4 = (bf16[512,3,1024]{2,0,1:T(8,128)(2,1)}, bf16[512,3,1024]{2,0,1:T(8,128)(2,1)S(1)}, u32[]{:S(2)}) copy-start(bf16[512,3,1024]{2,0,1:T(8,128)(2,1)S(1)} %collective-permute-done) | copy-start | bytes 9437188
  144.6 136.3 %collective-permute-start.2 = (bf16[512,3,1024]{2,0,1:T(8,128)(2,1)S(1)}, bf16[512,3,1024]{2,0,1:T(8,128)(2,1)S(1)}, u32[]{:S(2)}, u32[]{:S(2)}) collective-permute-start(bf16[512,3,1024]{2,0,1:T(8,128)(2,1)S(1)} %collective-permute-done), channel_id=1, source_target_pairs={{0,4},{4,8},{8,12},{12,16},{16,20},{20,24},{24,28},{28,0},{1,5},{5... | collective-permute-start | bytes 9437192 | tf_op jit(solution)/shard_map/ppermute | solution.py:16
  147.0 273.7 %copy-start.5 = (bf16[512,3,1024]{2,0,1:T(8,128)(2,1)}, bf16[512,3,1024]{2,0,1:T(8,128)(2,1)S(1)}, u32[]{:S(2)}) copy-start(bf16[512,3,1024]{2,0,1:T(8,128)(2,1)S(1)} %collective-permute-done.1) | copy-start | bytes 9437188
  147.0 138.0 %collective-permute-start.3 = (bf16[512,3,1024]{2,0,1:T(8,128)(2,1)S(1)}, bf16[512,3,1024]{2,0,1:T(8,128)(2,1)}, u32[]{:S(2)}, u32[]{:S(2)}) collective-permute-start(bf16[512,3,1024]{2,0,1:T(8,128)(2,1)S(1)} %collective-permute-done.1), channel_id=1, source_target_pairs={{0,28},{4,0},{8,4},{12,8},{16,12},{20,16},{24,20},{28,24},{1,29},{... | collective-permute-start | bytes 9437192 | tf_op jit(solution)/shard_map/ppermute | solution.py:21
  280.9 1.6 copy-start.3
  282.5 135.6 %collective-permute-start.4 = (bf16[512,3,1024]{2,0,1:T(8,128)(2,1)S(1)}, bf16[512,3,1024]{2,0,1:T(8,128)(2,1)}, u32[]{:S(2)}, u32[]{:S(2)}) collective-permute-start(bf16[512,3,1024]{2,0,1:T(8,128)(2,1)S(1)} %collective-permute-done.2), channel_id=1, source_target_pairs={{0,4},{4,8},{8,12},{12,16},{16,20},{20,24},{24,28},{28,0},{1,5},{5... | collective-permute-start | bytes 9437192 | tf_op jit(solution)/shard_map/ppermute | solution.py:16
  285.0 179.9 %collective-permute-start.5 = (bf16[512,3,1024]{2,0,1:T(8,128)(2,1)}, bf16[512,3,1024]{2,0,1:T(8,128)(2,1)}, u32[]{:S(2)}, u32[]{:S(2)}) collective-permute-start(bf16[512,3,1024]{2,0,1:T(8,128)(2,1)} %collective-permute-done.3), channel_id=1, source_target_pairs={{0,28},{4,0},{8,4},{12,8},{16,12},{20,16},{24,20},{28,24},{1,29},{... | collective-permute-start | bytes 9437192 | tf_op jit(solution)/shard_map/ppermute | solution.py:21
  418.1 71.6 %collective-permute-start.6 = (bf16[512,3,1024]{2,0,1:T(8,128)(2,1)}, bf16[512,3,1024]{2,0,1:T(8,128)(2,1)}, u32[]{:S(2)}, u32[]{:S(2)}) collective-permute-start(bf16[512,3,1024]{2,0,1:T(8,128)(2,1)} %collective-permute-done.4), channel_id=1, source_target_pairs={{0,4},{4,8},{8,12},{12,16},{16,20},{20,24},{24,28},{28,0},{1,5},{5... | collective-permute-start | bytes 9437192 | tf_op jit(solution)/shard_map/ppermute | solution.py:16
  469.5 3.0 copy-start.1
  538.0 6.2 copy-start.6
  538.0 140.4 %all-to-all-start = ((bf16[3,1024,768]{2,0,1:T(4,128)(2,1)}), bf16[3,1024,768]{2,0,1:T(4,128)(2,1)}, u32[]{:S(2)}, u32[]{:S(2)}) async-start(bf16[3,1024,768]{2,0,1:T(4,128)(2,1)} %copy.50), calls=%async_computation | async-start | bytes 12582912 | tf_op jit(solution)/shard_map/all_to_all | solution.py:87
  542.9 391.5 %reduce-scatter.2.cloned.1.call-start = ((), (), s32[]{:S(2)}) async-start(), calls=%async_computation.3 | async-start | bytes 15728640 | tf_op jit(solution)/shard_map/reduce_scatter | solution.py:96
  735.1 16.0 %copy-start = (f32[128,48,128]{2,1,0:T(8,128)S(1)}, f32[128,48,128]{2,1,0:T(8,128)}, u32[]{:S(2)}) copy-start(f32[128,48,128]{2,1,0:T(8,128)} %copy.57) | copy-start | bytes 9437188
  775.2 3.7 copy-start.2
Sparse Core Ops, SparseCore 0:
  836.2 98.1 reduce-scatter.1
